TPU v7x, 32 devices: a whole 2x2x4 slice. The times are simulated.
32 devices in a mesh: shot: 8 (over z, y), rcv: 4 (over x, core).
Axes of the slice: x: 2, y: 2, z: 4, core: 2. Of those that a mesh axis runs over, the one named last changes fastest.
Arguments:
- records: bfloat16 [1, 2, 1024, 8192], P(None, None, 'shot', 'rcv'), may hold values from -6 to 6
- aperture: int32 [1024, 2], P('shot'), may hold values from 0 to 3, all different within a row
- block_owner: int32 [4], replicated, may hold values from 0 to 7, as said below
- block_receivers: int32 [4, 128], replicated, may hold values from 0 to 8191, as said below
Outputs:
- multiples: bfloat16 [1, 2, 1024, 8192], P(None, None, 'shot', 'rcv')
Inputs may be any that keep to these rules, and one draw needn't show every extreme that they name: `block_owner`: distinct indices. `block_receivers`: distinct receivers.
All inputs are finite; a program needn't handle non-finite values.
Results may differ from a plain program's by a relative error of at most 0.001.
Values may be sent and summed in bfloat16 or wider, within the bound.
No kernel may reach another device: no remote copies, remote signals or barrier semaphores. Data moves between devices by JAX's collectives and lax.ppermute only.
A program may use at most 128 MiB of HBM per device.

v0:
```python
import jax
import jax.numpy as jnp
from jax import lax
from jax.sharding import PartitionSpec as P

APER = 2
BLOCK = 128


def broadcast(value, axis, source):
    kept = jnp.where(lax.axis_index(axis) == source, value, 0).astype(value.dtype)
    return lax.psum(kept, axis)


def complex_terms(block_portion, distant_offset):
    real_component = jnp.einsum(
        "uze,uew->uzw",
        block_portion[:, 0],
        distant_offset[:, 0],
        preferred_element_type=jnp.float32,
    ) - jnp.einsum(
        "uze,uew->uzw",
        block_portion[:, 1],
        distant_offset[:, 1],
        preferred_element_type=jnp.float32,
    )
    imag_part = jnp.einsum(
        "uze,uew->uzw",
        block_portion[:, 0],
        distant_offset[:, 1],
        preferred_element_type=jnp.float32,
    ) + jnp.einsum(
        "uze,uew->uzw",
        block_portion[:, 1],
        distant_offset[:, 0],
        preferred_element_type=jnp.float32,
    )
    return (real_component, imag_part)


def per_device(records, aperture, block_owner, block_receivers):
    freqs, parts, shots_here, rcv_here = records.shape
    nblocks, block_extent = block_receivers.shape
    first_rcv = lax.axis_index("rcv") * rcv_here
    requested_rows = block_receivers.reshape(1, -1)
    column_ids = first_rcv + lax.broadcasted_iota(jnp.int32, (rcv_here, 1), 0)
    selector = (column_ids == requested_rows).astype(jnp.bfloat16)
    local_cols = jnp.einsum("fcsr,rx->fcsx", records, selector, preferred_element_type=jnp.float32)
    near = lax.psum(local_cols.astype(jnp.bfloat16), "rcv")
    blocks = lax.broadcasted_iota(jnp.int32, (1, 1, nblocks), 2)
    use = jnp.any(aperture[:, :, None] == blocks, axis=1).astype(jnp.bfloat16)
    masked = (
        near.reshape(freqs, parts, shots_here, nblocks, block_extent) * use[None, None, :, :, None]
    )
    masked = masked.reshape(freqs, parts, shots_here, nblocks * block_extent)

    def fetch(block):
        return broadcast(records, "shot", block_owner[block])

    real_total = jnp.zeros((freqs, shots_here, rcv_here), jnp.float32)
    imaginary_total = jnp.zeros((freqs, shots_here, rcv_here), jnp.float32)
    gathered_rows = [fetch(block) for block in range(nblocks)]
    for block in range(nblocks):
        block_portion = masked[:, :, :, block * block_extent : (block + 1) * block_extent]
        real_component, imag_part = complex_terms(block_portion, gathered_rows[block])
        real_total = real_total + real_component
        imaginary_total = imaginary_total + imag_part
    factor = (2.0 * APER * BLOCK) ** (-0.5)
    return (jnp.stack([real_total, imaginary_total], axis=1) * factor).astype(jnp.bfloat16)


def solution(mesh):
    placed = (P(None, None, "shot", "rcv"), P("shot", None), P(), P())
    return jax.shard_map(
        per_device,
        mesh=mesh,
        in_specs=placed,
        out_specs=P(None, None, "shot", "rcv"),
        check_vma=False,
    )
```

profile of v0, /device:TPU:0, one launch (start us, length us, event | category | flops | bytes accessed | tf_op | source)
XLA Modules:
  0.0 222.4 jit_solution(10446118807844659125)
XLA Ops:
  6.5 0.0 all-reduce.4.cloned.1.call-start
  6.5 0.0 copy-start.5
  6.5 0.0 copy-start.4
  6.6 2.8 %fusion.17 = bf16[1,2,128,512]{2,3,1,0:T(8,128)(2,1)} fusion(s32[2048]{0:T(1024)S(1)} %iota_add_fusion, s32[512]{0:T(512)} %bitcast.89, bf16[1,2,128,2048]{3,2,1,0:T(8,128)(2,1)} %param.4), kind=kOutput, calls=%fused_computation.24 | convolution fusion | flops 538050560 | bytes 1320960 | tf_op jit(solution)/shard_map/fcsr,rx->fcsx/dot_general | solution.py:48
  9.4 0.0 all-reduce.4.cloned.1.call-update
  9.4 0.0 all-reduce.6.cloned.1.call-start
  9.4 0.0 copy-done.5
  9.4 0.7 fusion.30
  12.7 0.0 copy-done.4
  12.7 2.1 broadcast_select_fusion
  14.8 0.0 copy-start.6
  14.8 0.0 all-reduce.6.cloned.1.call-update
  14.8 0.7 copy-done.6
  15.5 29.2 %all-reduce.4.cloned.1.call-done = bf16[1,2,128,512]{2,3,1,0:T(8,128)(2,1)} async-done(((bf16[1,2,128,512]{2,3,1,0:T(8,128)(2,1)}), bf16[1,2,128,512]{2,3,1,0:T(8,128)(2,1)}) %all-reduce.4.cloned.1.call-update) | async-done | bytes 262160 | tf_op jit(solution)/shard_map/psum | solution.py:49
  44.7 1.0 broadcast_multiply_fusion
  45.7 159.6 %all-reduce.6.cloned.1.call-done = (bf16[1,2,128,2048]{3,2,1,0:T(8,128)(2,1)}, bf16[1,2,128,2048]{3,2,1,0:T(8,128)(2,1)}, bf16[1,2,128,2048]{3,2,1,0:T(8,128)(2,1)}, bf16[1,2,128,2048]{3,2,1,0:T(8,128)(2,1)}) async-done(((bf16[1,2,128,2048]{3,2,1,0:T(8,128)(2,1)}, bf16[1,2,128,2048]{3,2,1,0:T(8,128)(2,1)}, bf16[1,2,128,2048]{3,2,1,0:T(8,128)(2,1)}, bf16[1,2,128,2048]{3,2,1,0:T(8,128)(2,1)}), ...) | async-done | bytes 4194320 | tf_op jit(solution)/shard_map/psum | solution.py:12
  205.3 0.0 copy-start.3
  205.3 1.4 fusion.21
  206.7 0.0 copy-done.3
  206.7 0.0 copy-start.2
  206.7 0.3 fusion.22
  207.1 0.9 copy-done.2
  208.0 0.3 fusion.23
  208.3 0.0 copy-start.1
  208.3 0.3 fusion.24
  208.6 0.9 copy-done.1
  209.5 0.3 fusion.25
  209.8 0.0 copy-start
  209.9 0.3 fusion.26
  210.2 0.9 copy-done
  211.1 0.3 fusion.27
  211.4 0.3 fusion.28
  211.7 0.3 convolution_subtract_fusion.3
  212.0 0.3 convolution_add_fusion.3
  212.4 0.3 fusion.10
  212.7 0.3 fusion.9
  213.1 0.3 fusion.8
  213.4 0.3 fusion.6
  213.7 0.3 fusion.5
  214.1 0.3 fusion.4
  214.4 1.2 fusion.11
  (4 shorter events, 0.0 us)
Async XLA Ops:
  6.5 38.2 %all-reduce.4.cloned.1.call-start = ((), (), s32[]{:S(2)}) async-start(), calls=%async_computation | async-start | bytes 524288 | tf_op jit(solution)/shard_map/psum | solution.py:49
  6.5 2.9 %copy-start.5 = (s32[4]{0:T(128)S(1)}, s32[4]{0:T(128)}, u32[]{:S(2)}) copy-start(s32[4]{0:T(128)} %param.6) | copy-start | bytes 52
  6.5 6.2 %copy-start.4 = (bf16[1,2,128,2048]{3,2,1,0:T(8,128)(2,1)S(1)}, bf16[1,2,128,2048]{3,2,1,0:T(8,128)(2,1)}, u32[]{:S(2)}) copy-start(bf16[1,2,128,2048]{3,2,1,0:T(8,128)(2,1)} %param.4) | copy-start | bytes 3145732
  9.4 195.9 %all-reduce.6.cloned.1.call-start = ((), (), s32[]{:S(2)}) async-start(), calls=%async_computation.1 | async-start | bytes 8388608 | tf_op jit(solution)/shard_map/psum | solution.py:12
  14.8 0.7 copy-start.6
  205.3 1.5 copy-start.3
  206.7 1.2 copy-start.2
  208.3 1.2 copy-start.1
  209.8 1.2 copy-start
Sparse Core Ops, SparseCore 0:
  9.7 34.9 all-reduce.3
  48.7 156.4 all-reduce.5
where the time goes:
time: 223 us; the launch traced here: 222 us
  waiting for transfers between devices  189 us (85%)
  between operations  16.1 us (7%)
  matrix products  9.14 us (4%)
  other arithmetic  4.27 us (2%)
  local copies, waits for them, and re-layouts  4.04 us (2%)
    psum x1, waiting for transfers between devices, broadcast(): return lax.psum(kept, axis)  160 us
    psum x1, waiting for transfers between devices, per_device(): near = lax.psum(local_cols.astype(jnp.bfloat16), 'rcv')  29.2 us
  transfers between devices with their start and end apart: 2, of which 2 were waited for; matrix products, arithmetic and copies ran while one was open for 2% of the time, Pallas kernels for 0%

commit v1 on v0

--- a/solution.py
+++ b/solution.py
@@ -9,7 +9,7 @@
 
 def broadcast(value, axis, source):
     kept = jnp.where(lax.axis_index(axis) == source, value, 0).astype(value.dtype)
-    return lax.psum(kept, axis)
+    return jnp.sum(lax.all_gather(kept, axis), axis=0)
 
 
 def complex_terms(block_portion, distant_offset):

time: 223 us -> 537 us (2.41)
  waiting for transfers between devices: 189 us -> 475 us
  other arithmetic: 4.27 us -> 25.1 us
  matrix products: 9.14 us -> 15.7 us
    all_gather x0 -> x4, waiting for transfers between devices: none -> 447 us  [broadcast(): return jnp.sum(lax.all_gather(kept, axis), axis=0)]
    psum x1 -> x0, waiting for transfers between devices: 160 us -> none  [broadcast(): return lax.psum(kept, axis)]
    reduce_sum x0 -> x4, other arithmetic: none -> 20.9 us  [broadcast(): return jnp.sum(lax.all_gather(kept, axis), axis=0)]
  transfers between devices with their start and end apart: 2 -> 5, of which waited for: 2 -> 5; matrix products, arithmetic and copies ran while one was open for 2% -> 5% of each run, Pallas kernels for 0% -> 0%
where the time goes in v1:
time: 537 us; the launch traced here: 536 us
  waiting for transfers between devices  475 us (88%)
  other arithmetic  25.1 us (5%)
  between operations  17.9 us (3%)
  matrix products  15.7 us (3%)
    all_gather x4, waiting for transfers between devices, broadcast(): return jnp.sum(lax.all_gather(kept, axis), axis=0)  447 us
    psum x1, waiting for transfers between devices, per_device(): near = lax.psum(local_cols.astype(jnp.bfloat16), 'rcv')  27.1 us
    reduce_sum x4, other arithmetic, broadcast(): return jnp.sum(lax.all_gather(kept, axis), axis=0)  20.9 us
  transfers between devices with their start and end apart: 5, of which 5 were waited for; matrix products, arithmetic and copies ran while one was open for 5% of the time, Pallas kernels for 0%

profile of v1, /device:TPU:0, one launch (start us, length us, event | category | flops | bytes accessed | tf_op | source)
XLA Modules:
  0.0 536.4 jit_solution(2586172083104466017)
XLA Ops:
  7.4 2.8 fusion.17
  10.2 0.0 all-reduce.2.cloned.1.call-update
  10.2 0.0 all-gather.11.cloned.1.call-start
  10.3 1.5 fusion.30
  14.3 0.0 copy-start.8
  14.3 2.1 broadcast_select_fusion
  16.4 0.0 all-gather.11.cloned.1.call-update
  16.5 0.0 all-gather.9.cloned.1.call-start
  16.5 0.5 all-gather.9.cloned.1.call-update
  17.1 0.0 all-gather.13.cloned.1.call-start
  17.1 0.5 all-gather.13.cloned.1.call-update
  17.6 0.0 all-gather.15.cloned.1.call-start
  17.7 0.7 all-gather.15.cloned.1.call-update
  18.4 0.0 copy-done.8
  18.4 27.1 %all-reduce.2.cloned.1.call-done = bf16[1,2,128,512]{2,3,1,0:T(8,128)(2,1)} async-done(((bf16[1,2,128,512]{2,3,1,0:T(8,128)(2,1)}), bf16[1,2,128,512]{2,3,1,0:T(8,128)(2,1)}) %all-reduce.2.cloned.1.call-update) | async-done | bytes 262160 | tf_op jit(solution)/shard_map/psum | solution.py:49
  45.5 1.0 broadcast_multiply_fusion
  46.5 96.9 %all-gather.11.cloned.1.call-done = bf16[8,2,128,2048]{3,2,1,0:T(8,128)(2,1)} async-done(((bf16[1,2,128,2048]{3,2,1,0:T(8,128)(2,1)}), bf16[8,2,128,2048]{3,2,1,0:T(8,128)(2,1)}) %all-gather.11.cloned.1.call-update) | async-done | bytes 8388624 | tf_op jit(solution)/shard_map/all_gather | solution.py:12
  143.5 5.2 reduce.9
  148.7 119.1 %all-gather.9.cloned.1.call-done = bf16[8,2,128,2048]{3,2,1,0:T(8,128)(2,1)} async-done(((bf16[1,2,128,2048]{3,2,1,0:T(8,128)(2,1)}), bf16[8,2,128,2048]{3,2,1,0:T(8,128)(2,1)}) %all-gather.9.cloned.1.call-update) | async-done | bytes 8388624 | tf_op jit(solution)/shard_map/all_gather | solution.py:12
  267.8 5.2 reduce.8
  273.0 0.0 copy-start
  273.0 119.1 %all-gather.13.cloned.1.call-done = bf16[8,2,128,2048]{3,2,1,0:T(8,128)(2,1)} async-done(((bf16[1,2,128,2048]{3,2,1,0:T(8,128)(2,1)}), bf16[8,2,128,2048]{3,2,1,0:T(8,128)(2,1)}) %all-gather.13.cloned.1.call-update) | async-done | bytes 8388624 | tf_op jit(solution)/shard_map/all_gather | solution.py:12
  392.2 5.2 reduce.10
  397.4 1.3 fusion.26
  398.7 1.4 fusion.25
  400.1 1.3 fusion.22
  401.4 0.0 copy-done
  401.4 1.4 fusion.21
  402.7 1.3 fusion.24
  404.1 1.3 fusion.23
  405.4 111.3 %all-gather.15.cloned.1.call-done = bf16[8,2,128,2048]{3,2,1,0:T(8,128)(2,1)} async-done(((bf16[1,2,128,2048]{3,2,1,0:T(8,128)(2,1)}), bf16[8,2,128,2048]{3,2,1,0:T(8,128)(2,1)}) %all-gather.15.cloned.1.call-update) | async-done | bytes 8388624 | tf_op jit(solution)/shard_map/all_gather | solution.py:12
  516.7 5.2 reduce.11
  521.9 0.0 copy-start.1
  521.9 0.0 copy-start.6
  521.9 0.0 copy-start.5
  521.9 0.3 fusion.28
  522.3 0.3 fusion.27
  522.6 2.0 convolution_add_fusion.3
  524.6 0.3 convolution_subtract_fusion.3
  525.0 0.3 fusion.6
  525.3 0.3 fusion.5
  525.6 0.5 copy-done.4
  526.2 0.3 fusion.10
  526.5 0.1 copy-done.2
  526.6 0.3 fusion.9
  526.9 0.3 fusion.4
  527.3 0.3 fusion.8
  527.6 1.2 fusion.11
  (14 shorter events, 0.1 us)
Async XLA Ops:
  7.4 6.9 %copy-start.7 = (bf16[1,2,128,2048]{3,2,1,0:T(8,128)(2,1)S(1)}, bf16[1,2,128,2048]{3,2,1,0:T(8,128)(2,1)}, u32[]{:S(2)}) copy-start(bf16[1,2,128,2048]{3,2,1,0:T(8,128)(2,1)} %param.4) | copy-start | bytes 3145732
  7.4 38.2 %all-reduce.2.cloned.1.call-start = ((), (), s32[]{:S(2)}) async-start(), calls=%async_computation | async-start | bytes 524288 | tf_op jit(solution)/shard_map/psum | solution.py:49
  10.2 133.3 %all-gather.11.cloned.1.call-start = ((), (), s32[]{:S(2)}) async-start(), calls=%async_computation.2 | async-start | bytes 9437184 | tf_op jit(solution)/shard_map/all_gather | solution.py:12
  14.3 4.0 copy-start.8
  16.5 251.4 %all-gather.9.cloned.1.call-start = ((), (), s32[]{:S(2)}) async-start(), calls=%async_computation.1 | async-start | bytes 9437184 | tf_op jit(solution)/shard_map/all_gather | solution.py:12
  17.1 375.1 %all-gather.13.cloned.1.call-start = ((), (), s32[]{:S(2)}) async-start(), calls=%async_computation.3 | async-start | bytes 9437184 | tf_op jit(solution)/shard_map/all_gather | solution.py:12
  17.6 499.1 %all-gather.15.cloned.1.call-start = ((), (), s32[]{:S(2)}) async-start(), calls=%async_computation.4 | async-start | bytes 9437184 | tf_op jit(solution)/shard_map/all_gather | solution.py:12
  273.0 128.3 %copy-start = (bf16[2,128,2048]{2,1,0:T(8,128)(2,1)}, bf16[2,128,2048]{2,1,0:T(8,128)(2,1)S(1)}, u32[]{:S(2)}) copy-start(bf16[2,128,2048]{2,1,0:T(8,128)(2,1)S(1)} %reduce.8) | copy-start | bytes 3145732
  521.9 2.7 copy-start.1
  521.9 2.7 copy-start.6
  521.9 3.0 copy-start.5
  522.6 2.7 copy-start.3
  524.9 1.2 copy-start.4
  525.3 1.3 copy-start.2
Sparse Core Ops, SparseCore 0:
  10.5 34.9 all-reduce.1
Sparse Core Ops, SparseCore 1:
  16.5 126.9 all-gather.10
  145.5 122.3 all-gather.8
  269.8 122.3 all-gather.12
  394.3 122.3 all-gather.14
